TPU v7x, 32 devices: a whole 2x2x4 slice. The times are simulated.
32 devices in a mesh: section: 2 (over core), dp: 16 (over z, y, x).
Axes of the slice: x: 2, y: 2, z: 4, core: 2. Of those that a mesh axis runs over, the one named last changes fastest.
Arguments:
- acts: bfloat16 [2, 16, 1, 64, 2, 2, 128], P('section', 'dp'), may hold values from -6 to 6
- preacts: bfloat16 [2, 16, 1, 64, 2, 2, 128], P('section', 'dp'), may hold values from -6 to 6
- top_grad: bfloat16 [16, 1, 64, 2, 2, 128], P('dp'), may hold values from -6 to 6
- weights: bfloat16 [2, 64, 1728], P('section'), may hold values from -0.21875 to 0.21875
- a_factor: bfloat16 [2, 1728, 1728], P('section', 'dp'), as said below
- g_factor: bfloat16 [2, 64, 64], P('section'), as said below
Outputs:
- act_grads: bfloat16 [2, 16, 1, 64, 2, 2, 128], P('section', 'dp')
- update: float32 [2, 1728, 64], P('section', 'dp')
- inverse: float32 [2, 1728, 1728], P('section', 'dp')
Inputs may be any that keep to these rules, and one draw needn't show every extreme that they name: `a_factor`: each matrix is symmetric and positive definite. `g_factor`: each matrix is symmetric and positive definite.
All inputs are finite; a program needn't handle non-finite values. Where the computation divides by a largest or mean magnitude, that divisor is 1e-20 or more.
Results may differ from a plain program's by a relative error of at most 0.006.
Values may be sent and summed in bfloat16 or wider, within the bound.
No kernel may reach another device: no remote copies, remote signals or barrier semaphores. Data moves between devices by JAX's collectives and lax.ppermute only.
A program may use at most 64 MiB of HBM per device.

v0:
```python
import jax
import jax.numpy as jnp
from jax import lax
from jax.sharding import PartitionSpec as P

KW = 3
MICRO = 1


def shifted(value, axis, steps):
    count = lax.axis_size(axis)
    first, last = (max(0, -steps), min(count, count - steps))
    return lax.ppermute(value, axis, [(source, source + steps) for source in range(first, last)])


def tap_offsets(kernel_width):
    middle = kernel_width // 2
    result = []
    for along_x in range(kernel_width):
        for along_y in range(kernel_width):
            for along_z in range(kernel_width):
                result.append((along_x - middle, along_y - middle, along_z - middle))
    return result


def taps_stack(volume, kernel_width, direction):
    middle = kernel_width // 2
    padded = jnp.pad(volume, ((0, 0), (middle, middle), (middle, middle), (middle, middle)))
    size_x, size_y, size_z = (volume.shape[1], volume.shape[2], volume.shape[3])
    pieces = []
    for off_x, off_y, off_z in tap_offsets(kernel_width):
        start_x = middle + direction * off_x
        start_y = middle + direction * off_y
        start_z = middle + direction * off_z
        pieces.append(
            padded[
                :,
                start_x : start_x + size_x,
                start_y : start_y + size_y,
                start_z : start_z + size_z,
            ]
        )
    stacked = jnp.stack(pieces, 0)
    return stacked.reshape(len(pieces) * volume.shape[0], size_x * size_y * size_z)


def back_input(grad_out, w_rows):
    columns = taps_stack(grad_out, KW, -1)
    summed = lax.dot_general(
        w_rows, columns, (((0,), (0,)), ((), ())), preferred_element_type=jnp.float32
    )
    return summed.astype(jnp.bfloat16).reshape(grad_out.shape)


def back_weight(volume, grad_out):
    columns = taps_stack(volume, KW, 1)
    flattened = grad_out.reshape(grad_out.shape[0], -1)
    return lax.dot_general(
        columns, flattened, (((1,), (1,)), ((), ())), preferred_element_type=jnp.float32
    )


def local_inverse(matrix):
    values = matrix.astype(jnp.float32)
    step_size = 1.0 / jnp.max(jnp.sum(jnp.abs(values), axis=1))
    identity = jnp.eye(matrix.shape[0], dtype=jnp.float32)
    resid0 = (identity - step_size * values).astype(jnp.bfloat16)
    resid1 = jnp.dot(resid0, resid0, preferred_element_type=jnp.float32).astype(jnp.bfloat16)
    cross_term = jnp.dot(resid1, resid0, preferred_element_type=jnp.float32)
    return step_size * (
        identity + resid0.astype(jnp.float32) + resid1.astype(jnp.float32) + cross_term
    )


def eye_rows(start_row, row_total, order_full):
    column_ids = lax.broadcasted_iota(jnp.int32, (row_total, order_full), 1)
    row_ids = lax.broadcasted_iota(jnp.int32, (row_total, order_full), 0)
    return (column_ids == start_row + row_ids).astype(jnp.float32)


def shards(acts, preacts, top_grad, weights, a_factor, g_factor):
    section_index = lax.axis_index("section")
    section_count = lax.axis_size("section")
    tick_count = MICRO + section_count - 1
    inputs = acts[0, 0]
    pre_values = preacts[0, 0]
    upper_grads = top_grad[0]
    channels = weights.shape[1]
    w_rows = weights[0].reshape(channels, -1, channels).transpose(1, 0, 2).reshape(-1, channels)
    zero_field = jnp.zeros(inputs.shape[1:], jnp.bfloat16)

    def one_tick(tick_index, carried):
        outgoing, stored_grads, stored_slopes = carried
        incoming = shifted(outgoing, "section", -1)
        micro_index = tick_index - (section_count - 1 - section_index)
        is_valid = jnp.logical_and(micro_index >= 0, micro_index < MICRO)
        clipped = jnp.clip(micro_index, 0, MICRO - 1)
        from_top = lax.dynamic_index_in_dim(upper_grads, clipped, 0, keepdims=False)
        arriving = jnp.where(section_index == section_count - 1, from_top, incoming)
        pre_now = lax.dynamic_index_in_dim(pre_values, clipped, 0, keepdims=False)
        grad_out = jnp.where(pre_now > 0, arriving, zero_field)
        sending = back_input(grad_out, w_rows)
        old_grad = lax.dynamic_index_in_dim(stored_grads, clipped, 0, keepdims=False)
        old_slope = lax.dynamic_index_in_dim(stored_slopes, clipped, 0, keepdims=False)
        stored_grads = lax.dynamic_update_index_in_dim(
            stored_grads, jnp.where(is_valid, sending, old_grad), clipped, 0
        )
        stored_slopes = lax.dynamic_update_index_in_dim(
            stored_slopes, jnp.where(is_valid, grad_out, old_slope), clipped, 0
        )
        return (sending, stored_grads, stored_slopes)

    start_state = (
        zero_field,
        jnp.zeros(inputs.shape, jnp.bfloat16),
        jnp.zeros(inputs.shape, jnp.bfloat16),
    )
    last_sent, stored_grads, stored_slopes = lax.fori_loop(0, tick_count, one_tick, start_state)
    local_grad = back_weight(inputs[0], stored_slopes[0])
    summed_grad = lax.psum(local_grad, "dp")
    mean_grad = summed_grad / lax.axis_size("dp")
    a_rows = a_factor[0]
    row_total = a_rows.shape[0]
    order_full = a_rows.shape[1]
    first_row = lax.axis_index("dp") * row_total
    local_max = jnp.max(jnp.sum(jnp.abs(a_rows.astype(jnp.float32)), axis=1))
    step_size = 1.0 / lax.pmax(local_max, "dp")
    own_eye = eye_rows(first_row, row_total, order_full)
    resid0 = (own_eye - step_size * a_rows.astype(jnp.float32)).astype(jnp.bfloat16)
    left_cols = resid0
    resid1 = jnp.dot(
        left_cols,
        lax.all_gather(resid0, "dp", axis=0, tiled=True),
        preferred_element_type=jnp.float32,
    ).astype(jnp.bfloat16)
    left_cols = resid1
    cross_term = jnp.dot(
        left_cols,
        lax.all_gather(resid0, "dp", axis=0, tiled=True),
        preferred_element_type=jnp.float32,
    )
    inverse_rows = step_size * (
        own_eye + resid0.astype(jnp.float32) + resid1.astype(jnp.float32) + cross_term
    )
    g_inverse = local_inverse(g_factor[0])
    preconditioned = jnp.dot(
        mean_grad, g_inverse, precision=lax.Precision.HIGHEST, preferred_element_type=jnp.float32
    )
    update_rows = jnp.dot(
        inverse_rows,
        preconditioned,
        precision=lax.Precision.HIGHEST,
        preferred_element_type=jnp.float32,
    )
    return (stored_grads[None, None], update_rows[None], inverse_rows[None])


def solution(mesh):
    placed = (
        P("section", "dp", None, None, None, None, None),
        P("section", "dp", None, None, None, None, None),
        P("dp", None, None, None, None, None),
        P("section", None, None),
        P("section", "dp", None),
        P("section", None, None),
    )
    return jax.shard_map(
        shards,
        mesh=mesh,
        in_specs=placed,
        out_specs=(
            P("section", "dp", None, None, None, None, None),
            P("section", "dp", None),
            P("section", "dp", None),
        ),
        check_vma=False,
    )
```

profile of v0, /device:TPU:0, one launch (start us, length us, event | category | flops | bytes accessed | tf_op | source)
XLA Modules:
  0.0 278.0 jit_solution(16409648565365553291)
XLA Ops:
  7.2 1.5 reshape_squeeze.6
  8.7 0.9 copy.18
  9.7 0.2 fusion.56
  10.8 0.2 fusion.82
  11.1 0.2 fusion.86
  11.7 0.2 fusion.92
  12.0 0.2 fusion.96
  13.2 2.1 reshape.70
  15.3 0.7 broadcast.39
  16.0 0.7 broadcast.40
  16.6 24.1 %while.20 = (s32[]{:T(128)}, bf16[64,2,2,128]{3,2,1,0:T(2,128)(2,1)}, bf16[1,64,2,2,128]{4,3,2,1,0:T(2,128)(2,1)}, bf16[1,64,2,2,128]{4,3,2,1,0:T(2,128)(2,1)}, ...) while((s32[]{:T(128)}, ...), condition=%wide.region_1.2_spmd.clone, body=%wide.region_0.1_spmd.clone.sunk | while | flops 113475592 | bytes 10772739 | solution.py:118
  16.6 1.3 collective-permute-start
  17.9 2.0 collective-permute-done
  20.0 1.7 fusion.173
  22.6 0.2 fusion.183
  22.9 0.2 fusion.185
  23.5 0.2 fusion.188
  23.8 0.2 fusion.190
  25.0 0.7 reshape.79
  25.7 1.5 fusion.200
  27.2 0.6 reshape.80
  28.0 0.6 copy-done.5
  28.6 1.3 collective-permute-start
  29.9 2.0 collective-permute-done
  32.0 1.7 fusion.173
  34.7 0.2 fusion.183
  35.0 0.2 fusion.185
  35.5 0.2 fusion.188
  35.8 0.2 fusion.190
  37.0 0.7 reshape.79
  37.8 1.5 fusion.200
  39.3 0.6 reshape.80
  40.1 0.6 copy-done.5
  40.7 0.9 reshape_squeeze.7
  41.6 0.6 reduce_max.18
  42.2 2.9 %fusion.129 = f32[1728,64]{0,1:T(8,128)} fusion(bf16[1728,512]{1,0:T(8,128)(2,1)} %reshape.70, bf16[64,512]{1,0:T(8,128)(2,1)S(1)} %reshape_squeeze.7), kind=kOutput, calls=%fused_computation.203 | convolution fusion | flops 113246208 | bytes 2277376 | tf_op jit(solution)/shard_map/dot_general | solution.py:58
  45.2 44.4 %pmax.7 = f32[]{:T(128)} all-reduce(f32[]{:T(128)} %reduce_max.18), channel_id=1, replica_groups=mesh['section'=2,'dp'=16] {'dp'}, use_global_device_ids=true, to_apply=%region_4.5 | all-reduce | flops 1 | bytes 8 | tf_op jit(solution)/shard_map/pmax | solution.py:127
  90.3 1.0 fusion.128
  91.4 0.6 reduce_max.19
  93.0 64.2 %all-reduce.4.cloned.1.call-done = f32[1728,64]{0,1:T(8,128)} async-done(((f32[1728,64]{0,1:T(8,128)}), f32[1728,64]{0,1:T(8,128)}) %all-reduce.4.cloned.1.call-update) | async-done | bytes 442384 | tf_op jit(solution)/shard_map/psum | solution.py:120
  157.1 1.6 fusion.60
  158.7 94.8 %all-gather.3.cloned.1.call-done = bf16[16,108,1728]{2,1,0:T(8,128)(2,1)} async-done(((bf16[1,108,1728]{2,1,0:T(8,128)(2,1)}), bf16[16,108,1728]{2,1,0:T(8,128)(2,1)}) %all-gather.3.cloned.1.call-update) | async-done | bytes 5971984 | tf_op jit(solution)/shard_map/all_gather | solution.py:133
  253.5 8.7 %reshape.72 = bf16[1728,1728]{1,0:T(8,128)(2,1)} reshape(bf16[16,108,1728]{2,1,0:T(8,128)(2,1)} %all-gather.3.cloned.1.call-done) | data formatting | bytes 11943936
  262.3 4.0 %convolution_convert_fusion.1 = bf16[108,1728]{1,0:T(8,128)(2,1)S(1)} fusion(bf16[1728,1728]{1,0:T(8,128)(2,1)} %reshape.72, bf16[1,108,1728]{2,1,0:T(8,128)(2,1)S(1)} %copy-done.3, f32[]{:T(128)S(6)} %div.12, s32[108]{0:T(128)S(1)} %iota_add_fusion), kind=kOutput, calls=%fused_computation.115 | convolution fusion | flops 646278912 | bytes 6718900 | tf_op jit(solution)/shard_map/dot_general | solution.py:131
  266.3 0.6 copy-done
  266.8 1.1 fusion.54
  267.9 1.6 convolution_bitcast_fusion
  269.5 1.7 copy.17
  (97 shorter events, 8.6 us)
Async XLA Ops:
  7.2 2.5 copy-start.2
  7.2 2.6 copy-start.1
  7.2 149.9 %all-reduce.4.cloned.1.call-start = ((), (), s32[]{:S(2)}) async-start(), calls=%async_computation | async-start | bytes 917504 | tf_op jit(solution)/shard_map/psum | solution.py:120
  16.6 3.3 %collective-permute-start = (bf16[64,2,2,128]{3,2,1,0:T(2,128)(2,1)}, bf16[64,2,2,128]{3,2,1,0:T(2,128)(2,1)S(1)}, u32[]{:S(2)}, u32[]{:S(2)}) collective-permute-start(bf16[64,2,2,128]{3,2,1,0:T(2,128)(2,1)} %get-tuple-element.362), channel_id=1, source_target_pairs={{16,0},{17,1},{18,2},{19,3},{20,4},{21,5},{22,6},{23,7},{24,8},{25... | collective-permute-start | bytes 196616 | tf_op jit(solution)/shard_map/while/body/eval_jaxpr/ppermute | solution.py:13
  25.7 2.2 copy-start.4
  28.0 0.6 copy-start.5
  28.6 3.3 %collective-permute-start = (bf16[64,2,2,128]{3,2,1,0:T(2,128)(2,1)}, bf16[64,2,2,128]{3,2,1,0:T(2,128)(2,1)S(1)}, u32[]{:S(2)}, u32[]{:S(2)}) collective-permute-start(bf16[64,2,2,128]{3,2,1,0:T(2,128)(2,1)} %get-tuple-element.362), channel_id=1, source_target_pairs={{16,0},{17,1},{18,2},{19,3},{20,4},{21,5},{22,6},{23,7},{24,8},{25... | collective-permute-start | bytes 196616 | tf_op jit(solution)/shard_map/while/body/eval_jaxpr/ppermute | solution.py:13
  37.8 2.2 copy-start.4
  40.1 0.6 copy-start.5
  40.7 49.6 %copy-start.3 = (bf16[1,108,1728]{2,1,0:T(8,128)(2,1)S(1)}, bf16[1,108,1728]{2,1,0:T(8,128)(2,1)}, u32[]{:S(2)}) copy-start(bf16[1,108,1728]{2,1,0:T(8,128)(2,1)} %param.12) | copy-start | bytes 1119748
  42.2 49.1 %copy-start.6 = (bf16[1,64,64]{2,1,0:T(8,128)(2,1)S(1)}, bf16[1,64,64]{2,1,0:T(8,128)(2,1)}, u32[]{:S(2)}) copy-start(bf16[1,64,64]{2,1,0:T(8,128)(2,1)} %param.13) | copy-start | bytes 24580
  45.1 208.4 %all-gather.3.cloned.1.call-start = ((), (), s32[]{:S(2)}) async-start(), calls=%async_computation.1 | async-start | bytes 6823936 | tf_op jit(solution)/shard_map/all_gather | solution.py:133
  262.3 4.5 %copy-start = (bf16[1728,1728]{1,0:T(8,128)(2,1)S(1)}, bf16[1728,1728]{1,0:T(8,128)(2,1)}, u32[]{:S(2)}) copy-start(bf16[1728,1728]{1,0:T(8,128)(2,1)} %reshape.72) | copy-start | bytes 17915908
Sparse Core Ops, SparseCore 0:
  45.3 111.8 all-reduce.3
  159.9 93.6 all-gather.2
where the time goes:
time: 279 us; the launch traced here: 278 us
  waiting for transfers between devices  163 us (58%)
  blocking collectives  44.4 us (16%)
  local copies, waits for them, and re-layouts  31.8 us (11%)
  between operations  15.5 us (6%)
  matrix products  14.4 us (5%)
  other arithmetic  6.04 us (2%)
    all_gather x1, waiting for transfers between devices, shards(): lax.all_gather(resid0, 'dp', axis=0, tiled=True)  94.8 us
    psum x1, waiting for transfers between devices, shards(): summed_grad = lax.psum(local_grad, 'dp')  64.2 us
    pmax x1, blocking collectives, shards(): step_size = 1.0 / lax.pmax(local_max, 'dp')  44.4 us
    unnamed x39, local copies, waits for them, and re-layouts  15.1 us
    while x60, local copies, waits for them, and re-layouts  7.65 us
  transfers between devices with their start and end apart: 4, of which 4 were waited for; matrix products, arithmetic and copies ran while one was open for 1% of the time, Pallas kernels for 0%

commit v1 on v0

--- a/solution.py
+++ b/solution.py
@@ -117,7 +117,11 @@
     )
     last_sent, stored_grads, stored_slopes = lax.fori_loop(0, tick_count, one_tick, start_state)
     local_grad = back_weight(inputs[0], stored_slopes[0])
-    summed_grad = lax.psum(local_grad, "dp")
+    summed_grad = local_grad
+    for hop in (1, 2, 4, 8):
+        summed_grad = summed_grad + lax.ppermute(
+            summed_grad, "dp", [(dev, dev ^ hop) for dev in range(16)]
+        )
     mean_grad = summed_grad / lax.axis_size("dp")
     a_rows = a_factor[0]
     row_total = a_rows.shape[0]

time: 279 us -> 205 us (0.73)
  waiting for transfers between devices: 163 us -> 85.5 us
  starting transfers between devices: 2.64 us -> 9.19 us
  local copies, waits for them, and re-layouts: 31.8 us -> 28.9 us
    all_gather x1, waiting for transfers between devices: 94.8 us -> 0.02 us  [shards(): lax.all_gather(resid0, 'dp', axis=0, tiled=True)]
    ppermute x0 -> x4, waiting for transfers between devices: none -> 81.7 us  [shards(): lax.ppermute(summed_grad, 'dp', [(dev, dev ^ hop) for dev in range(16)])]
    psum x1 -> x0, waiting for transfers between devices: 64.2 us -> none  [shards(): summed_grad = lax.psum(local_grad, 'dp')]
    ppermute x0 -> x4, starting transfers between devices: none -> 6.59 us  [shards(): lax.ppermute(summed_grad, 'dp', [(dev, dev ^ hop) for dev in range(16)])]
  transfers between devices with their start and end apart: 4 -> 7, of which waited for: 4 -> 6; matrix products, arithmetic and copies ran while one was open for 1% -> 13% of each run, Pallas kernels for 0% -> 0%
where the time goes in v1:
time: 205 us; the launch traced here: 204 us
  waiting for transfers between devices  85.5 us (42%)
  blocking collectives  44.1 us (22%)
  local copies, waits for them, and re-layouts  28.9 us (14%)
  between operations  15.6 us (8%)
  matrix products  12.6 us (6%)
  starting transfers between devices  9.19 us (4%)
  other arithmetic  8.32 us (4%)
    ppermute x4, waiting for transfers between devices, shards(): lax.ppermute(summed_grad, 'dp', [(dev, dev ^ hop) for dev in range(16)])  81.7 us
    pmax x1, blocking collectives, shards(): step_size = 1.0 / lax.pmax(local_max, 'dp')  44.1 us
    unnamed x39, local copies, waits for them, and re-layouts  15.2 us
    while x60, local copies, waits for them, and re-layouts  7.65 us
    ppermute x4, starting transfers between devices, shards(): lax.ppermute(summed_grad, 'dp', [(dev, dev ^ hop) for dev in range(16)])  6.59 us
    dot_general x2, matrix products, shards(): jnp.dot(left_cols, lax.all_gather(resid0, 'dp', axis=0, tiled=True), pref...  5.03 us
  transfers between devices with their start and end apart: 7, of which 6 were waited for; matrix products, arithmetic and copies ran while one was open for 13% of the time, Pallas kernels for 0%

profile of v1, /device:TPU:0, one launch (start us, length us, event | category | flops | bytes accessed | tf_op | source)
XLA Modules:
  0.0 204.3 jit_solution(304830258781279002)
XLA Ops:
  7.2 1.3 fusion.56
  8.5 0.6 reduce_max.18
  9.1 44.1 %pmax.7 = f32[]{:T(128)} all-reduce(f32[]{:T(128)} %reduce_max.18), channel_id=1, replica_groups=mesh['section'=2,'dp'=16] {'dp'}, use_global_device_ids=true, to_apply=%region_4.5 | all-reduce | flops 1 | bytes 8 | tf_op jit(solution)/shard_map/pmax | solution.py:131
  53.9 2.0 fusion.129
  56.0 0.5 reshape_squeeze.6
  56.5 0.9 copy.18
  58.4 0.2 fusion.83
  58.7 0.2 fusion.87
  59.3 0.2 fusion.93
  59.6 0.2 fusion.97
  60.8 2.1 %reshape.70 = bf16[1728,512]{1,0:T(8,128)(2,1)} reshape(bf16[27,64,2,2,128]{4,3,2,1,0:T(2,128)(2,1)S(1)} %fusion.115) | data formatting | bytes 3538944 | tf_op jit(solution)/shard_map/reshape | solution.py:44
  62.9 0.7 broadcast.40
  63.6 22.4 %while.20 = (s32[]{:T(128)}, bf16[64,2,2,128]{3,2,1,0:T(2,128)(2,1)S(1)}, bf16[1,64,2,2,128]{4,3,2,1,0:T(2,128)(2,1)}, bf16[1,64,2,2,128]{4,3,2,1,0:T(2,128)(2,1...) while((s32[]{:T(128)}, ...), condition=%wide.region_1.2_spmd.clone, body=%wide.region_0.1_spmd.clone.sunk | while | flops 113475592 | bytes 10772739 | solution.py:118
  63.6 1.3 collective-permute-start
  64.9 1.8 collective-permute-done
  66.7 1.7 fusion.174
  69.4 0.2 fusion.184
  69.7 0.2 fusion.186
  70.2 0.2 fusion.189
  70.5 0.2 fusion.191
  71.7 0.7 reshape.79
  72.5 1.5 fusion.201
  74.1 0.6 copy-done.4
  74.8 1.3 collective-permute-start
  76.1 1.8 collective-permute-done
  77.9 1.7 fusion.174
  80.6 0.2 fusion.184
  81.4 0.2 fusion.189
  82.9 0.7 reshape.79
  83.7 1.5 fusion.201
  85.4 0.6 copy-done.4
  86.0 0.9 reshape_squeeze.7
  86.9 2.1 %fusion.130 = f32[1728,64]{0,1:T(8,128)S(1)} fusion(bf16[1728,512]{1,0:T(8,128)(2,1)} %reshape.70, bf16[64,512]{1,0:T(8,128)(2,1)S(1)} %reshape_squeeze.7), kind=kOutput, calls=%fused_computation.204 | convolution fusion | flops 113246208 | bytes 2277376 | tf_op jit(solution)/shard_map/dot_general | solution.py:58
  89.1 14.0 %collective-permute-done.1 = f32[1728,64]{0,1:T(8,128)S(1)} collective-permute-done((f32[1728,64]{0,1:T(8,128)S(1)}, f32[1728,64]{0,1:T(8,128)S(1)}, u32[]{:S(2)}, u32[]{:S(2)}) %collective-permute-start.1) | collective-permute-done | bytes 442400 | tf_op jit(solution)/shard_map/ppermute | solution.py:122
  103.1 1.5 collective-permute-start.2
  104.6 10.8 %collective-permute-done.2 = f32[1728,64]{0,1:T(8,128)S(1)} collective-permute-done((f32[1728,64]{0,1:T(8,128)S(1)}, f32[1728,64]{0,1:T(8,128)S(1)}, u32[]{:S(2)}, u32[]{:S(2)}) %collective-permute-start.2) | collective-permute-done | bytes 442400 | tf_op jit(solution)/shard_map/ppermute | solution.py:122
  115.5 1.6 collective-permute-start.3
  117.2 0.6 reduce_max.19
  118.5 34.3 %collective-permute-done.3 = f32[1728,64]{0,1:T(8,128)S(1)} collective-permute-done((f32[1728,64]{0,1:T(8,128)S(1)}, f32[1728,64]{0,1:T(8,128)S(1)}, u32[]{:S(2)}, u32[]{:S(2)}) %collective-permute-start.3) | collective-permute-done | bytes 442400 | tf_op jit(solution)/shard_map/ppermute | solution.py:122
  152.9 3.4 %collective-permute-start.4 = (f32[1728,64]{0,1:T(8,128)S(1)}, f32[1728,64]{0,1:T(8,128)S(1)}, u32[]{:S(2)}, u32[]{:S(2)}) collective-permute-start(f32[1728,64]{0,1:T(8,128)S(1)} %add.78), channel_id=1, source_target_pairs={{0,8},{1,9},{2,10},{3,11},{4,12},{5,13},{6,14},{7,15},{8,0},{9,1},... | collective-permute-start | bytes 1327112 | tf_op jit(solution)/shard_map/ppermute | solution.py:122
  156.6 22.6 %collective-permute-done.4 = f32[1728,64]{0,1:T(8,128)S(1)} collective-permute-done((f32[1728,64]{0,1:T(8,128)S(1)}, f32[1728,64]{0,1:T(8,128)S(1)}, u32[]{:S(2)}, u32[]{:S(2)}) %collective-permute-start.4) | collective-permute-done | bytes 442400 | tf_op jit(solution)/shard_map/ppermute | solution.py:122
  179.2 0.6 fusion.60
  179.8 8.8 %reshape.72 = bf16[1728,1728]{1,0:T(8,128)(2,1)} reshape(bf16[16,108,1728]{2,1,0:T(8,128)(2,1)} %all-gather.3.cloned.1.call-done) | data formatting | bytes 11943936
  188.6 4.0 %convolution_convert_fusion.1 = bf16[108,1728]{1,0:T(8,128)(2,1)S(1)} fusion(bf16[1728,1728]{1,0:T(8,128)(2,1)} %reshape.72, bf16[1,108,1728]{2,1,0:T(8,128)(2,1)S(1)} %copy-done.2, f32[]{:T(128)S(6)} %div.12, s32[108]{0:T(128)S(1)} %iota_add_fusion), kind=kOutput, calls=%fused_computation.115 | convolution fusion | flops 646278912 | bytes 6718900 | tf_op jit(solution)/shard_map/dot_general | solution.py:135
  192.6 0.6 copy-done
  193.1 1.1 fusion.54
  194.2 1.6 convolution_bitcast_fusion
  195.8 1.7 copy.17
  (105 shorter events, 9.2 us)
Async XLA Ops:
  7.2 48.8 %copy-start.5 = (bf16[1,64,1728]{2,1,0:T(8,128)(2,1)S(1)}, bf16[1,64,1728]{2,1,0:T(8,128)(2,1)}, u32[]{:S(2)}) copy-start(bf16[1,64,1728]{2,1,0:T(8,128)(2,1)} %param.11) | copy-start | bytes 663556
  7.2 50.2 %copy-start.1 = (bf16[1,1,1,64,2,2,128]{6,5,4,3,2,1,0:T(2,128)(2,1)S(1)}, bf16[1,1,1,64,2,2,128]{6,5,4,3,2,1,0:T(2,128)(2,1)}, u32[]{:S(2)}) copy-start(bf16[1,1,1,64,2,2,128]{6,5,4,3,2,1,0:T(2,128)(2,1)} %param.8) | copy-start | bytes 196612
  7.2 172.6 %all-gather.3.cloned.1.call-start = ((), (), s32[]{:S(2)}) async-start(), calls=%async_computation | async-start | bytes 6823936 | tf_op jit(solution)/shard_map/all_gather | solution.py:137
  63.6 3.1 %collective-permute-start = (bf16[64,2,2,128]{3,2,1,0:T(2,128)(2,1)S(1)}, bf16[64,2,2,128]{3,2,1,0:T(2,128)(2,1)S(1)}, u32[]{:S(2)}, u32[]{:S(2)}) collective-permute-start(bf16[64,2,2,128]{3,2,1,0:T(2,128)(2,1)S(1)} %get-tuple-element.362), channel_id=1, source_target_pairs={{16,0},{17,1},{18,2},{19,3},{20,4},{21,5},{22,6},{23,7},{24,8},{25... | collective-permute-start | bytes 196616 | tf_op jit(solution)/shard_map/while/body/eval_jaxpr/ppermute | solution.py:13
  72.4 1.6 copy-start.3
  74.1 0.6 copy-start.4
  74.8 3.1 %collective-permute-start = (bf16[64,2,2,128]{3,2,1,0:T(2,128)(2,1)S(1)}, bf16[64,2,2,128]{3,2,1,0:T(2,128)(2,1)S(1)}, u32[]{:S(2)}, u32[]{:S(2)}) collective-permute-start(bf16[64,2,2,128]{3,2,1,0:T(2,128)(2,1)S(1)} %get-tuple-element.362), channel_id=1, source_target_pairs={{16,0},{17,1},{18,2},{19,3},{20,4},{21,5},{22,6},{23,7},{24,8},{25... | collective-permute-start | bytes 196616 | tf_op jit(solution)/shard_map/while/body/eval_jaxpr/ppermute | solution.py:13
  83.7 1.6 copy-start.3
  85.3 0.6 copy-start.4
  89.0 28.1 %copy-start.6 = (bf16[1,64,64]{2,1,0:T(8,128)(2,1)S(1)}, bf16[1,64,64]{2,1,0:T(8,128)(2,1)}, u32[]{:S(2)}) copy-start(bf16[1,64,64]{2,1,0:T(8,128)(2,1)} %param.13) | copy-start | bytes 24580
  89.0 14.1 %collective-permute-start.1 = (f32[1728,64]{0,1:T(8,128)S(1)}, f32[1728,64]{0,1:T(8,128)S(1)}, u32[]{:S(2)}, u32[]{:S(2)}) collective-permute-start(f32[1728,64]{0,1:T(8,128)S(1)} %fusion.130), channel_id=1, source_target_pairs={{0,1},{1,0},{2,3},{3,2},{4,5},{5,4},{6,7},{7,6},{8,9},{9,8},{10,11... | collective-permute-start | bytes 1327112 | tf_op jit(solution)/shard_map/ppermute | solution.py:122
  103.1 12.4 %collective-permute-start.2 = (f32[1728,64]{0,1:T(8,128)S(1)}, f32[1728,64]{0,1:T(8,128)S(1)}, u32[]{:S(2)}, u32[]{:S(2)}) collective-permute-start(f32[1728,64]{0,1:T(8,128)S(1)} %add.76), channel_id=1, source_target_pairs={{0,2},{1,3},{2,0},{3,1},{4,6},{5,7},{6,4},{7,5},{8,10},{9,11},{10,... | collective-permute-start | bytes 1327112 | tf_op jit(solution)/shard_map/ppermute | solution.py:122
  115.5 37.3 %collective-permute-start.3 = (f32[1728,64]{0,1:T(8,128)S(1)}, f32[1728,64]{0,1:T(8,128)S(1)}, u32[]{:S(2)}, u32[]{:S(2)}) collective-permute-start(f32[1728,64]{0,1:T(8,128)S(1)} %add.77), channel_id=1, source_target_pairs={{0,4},{1,5},{2,6},{3,7},{4,0},{5,1},{6,2},{7,3},{8,12},{9,13},{10,... | collective-permute-start | bytes 1327112 | tf_op jit(solution)/shard_map/ppermute | solution.py:122
  152.9 26.3 %collective-permute-start.4 = (f32[1728,64]{0,1:T(8,128)S(1)}, f32[1728,64]{0,1:T(8,128)S(1)}, u32[]{:S(2)}, u32[]{:S(2)}) collective-permute-start(f32[1728,64]{0,1:T(8,128)S(1)} %add.78), channel_id=1, source_target_pairs={{0,8},{1,9},{2,10},{3,11},{4,12},{5,13},{6,14},{7,15},{8,0},{9,1},... | collective-permute-start | bytes 1327112 | tf_op jit(solution)/shard_map/ppermute | solution.py:122
  179.7 8.8 %copy-start.2 = (bf16[1,108,1728]{2,1,0:T(8,128)(2,1)S(1)}, bf16[1,108,1728]{2,1,0:T(8,128)(2,1)}, u32[]{:S(2)}) copy-start(bf16[1,108,1728]{2,1,0:T(8,128)(2,1)} %param.12) | copy-start | bytes 1119748
  188.6 4.5 %copy-start = (bf16[1728,1728]{1,0:T(8,128)(2,1)S(1)}, bf16[1728,1728]{1,0:T(8,128)(2,1)}, u32[]{:S(2)}) copy-start(bf16[1728,1728]{1,0:T(8,128)(2,1)} %reshape.72) | copy-start | bytes 17915908
Sparse Core Ops, SparseCore 0:
  56.1 110.5 all-gather.2
